TPU v7x, 512 devices: a whole 4x4x16 slice. The times are simulated.
512 devices in a mesh: ctx: 64 (over z, y), head: 8 (over x, core).
Axes of the slice: x: 4, y: 4, z: 16, core: 2. Of those that a mesh axis runs over, the one named last changes fastest.
Arguments:
- queries: bfloat16 [8192, 4096], P(('ctx', 'head')), may hold values from -4.6 to 4.6
- key_states: bfloat16 [8192, 4096], P(('ctx', 'head')), may hold values from -4.6 to 4.6
- value_states: bfloat16 [8192, 4096], P(('ctx', 'head')), may hold values from -6 to 6
- out_grad: bfloat16 [8192, 4096], P(('ctx', 'head')), may hold values from -6 to 6
- random_blocks: int32 [256, 3], replicated, may hold values from 0 to 255, as said below
- global_blocks: int32 [4], replicated, may hold values from 0 to 255, as said below
Outputs:
- query_grad: bfloat16 [8192, 4096], P('ctx', 'head')
- key_grad: bfloat16 [8192, 4096], P('ctx', 'head')
- value_grad: bfloat16 [8192, 4096], P('ctx', 'head')
Inputs may be any that keep to these rules, and one draw needn't show every extreme that they name: `random_blocks`: with the blocks i * 4 to i * 4 + 3 called range i: the 12 entries of the rows of range i name blocks of any one range at most 1 times, and some range exactly 1 times. `global_blocks`: 4 different blocks, one of them the last block 255, in any order.
All inputs are finite; a program needn't handle non-finite values.
Results may differ from a plain program's by a relative error of at most 0.0077.
Values may be sent and summed in bfloat16 or wider, within the bound.
No kernel may reach another device: no remote copies, remote signals or barrier semaphores. Data moves between devices by JAX's collectives and lax.ppermute only.
A program may use at most 128 MiB of HBM per device.

v0:
```python
import math
import jax
import jax.numpy as jnp
from jax import lax
from jax.sharding import PartitionSpec as P

DH = 128
BS = 32
NR = 3
NG = 4


def with_halo(x, sides, width):
    for axis, dim in sides:
        peers, length = (lax.axis_size(axis), x.shape[dim])
        up = [(i, (i + 1) % peers) for i in range(peers - 1)]
        down = [(j, i) for i, j in up]
        last = lax.slice_in_dim(x, length - width, length, axis=dim)
        first = lax.slice_in_dim(x, 0, width, axis=dim)
        before = lax.ppermute(last, axis, up)
        after = lax.ppermute(first, axis, down)
        x = jnp.concatenate([before, x, after], axis=dim)
    return x


def spread(x, axis, root):
    mine = lax.axis_index(axis) == root
    return lax.psum(jnp.where(mine, x, jnp.zeros_like(x)), axis)


def per_device(queries, key_states, value_states, out_grad, random_blocks, global_blocks):
    query_rows, key_rows, value_rows, grad_rows = (
        lax.all_to_all(queries, "head", split_axis=1, concat_axis=0, tiled=True),
        lax.all_to_all(key_states, "head", split_axis=1, concat_axis=0, tiled=True),
        lax.all_to_all(value_states, "head", split_axis=1, concat_axis=0, tiled=True),
        lax.all_to_all(out_grad, "head", split_axis=1, concat_axis=0, tiled=True),
    )
    tokens = query_rows.shape[0]
    head_cols = query_rows.shape[1]
    heads_here = head_cols // DH
    blocks_here = tokens // BS
    devices = lax.axis_size("ctx")
    my_index = lax.axis_index("ctx")
    total_blocks = devices * blocks_here
    entries = blocks_here * NR
    capacity = (entries + devices - 1) // devices
    inv_root = 1.0 / math.sqrt(DH)
    kv_rows = jnp.concatenate([key_rows, value_rows], axis=1)
    kv_blocks = kv_rows.reshape(blocks_here, BS, 2 * head_cols)
    extended = with_halo(kv_rows, (("ctx", 0),), BS)
    extended = extended.reshape(blocks_here + 2, BS, 2 * head_cols)
    window = jnp.stack(
        [extended[:blocks_here], extended[1 : blocks_here + 1], extended[2:]], axis=1
    )
    global_owner = global_blocks // blocks_here
    global_offset = global_blocks % blocks_here
    pieces = []
    for member in range(NG):
        own_block = lax.dynamic_index_in_dim(kv_blocks, global_offset[member], 0, keepdims=False)
        pieces.append(spread(own_block, "ctx", global_owner[member]))
    global_kv = jnp.stack(pieces)
    entry_table = random_blocks.reshape(devices, entries)
    table_owner = entry_table // blocks_here
    table_offset = entry_table % blocks_here
    positions = jnp.arange(entries, dtype=jnp.int32)
    before = positions[None, :] < positions[:, None]
    matches = (table_owner[:, :, None] == table_owner[:, None, :]) & before[None]
    table_slot = jnp.sum(matches.astype(jnp.int32), axis=2)
    my_owner = lax.dynamic_index_in_dim(table_owner, my_index, 0, keepdims=False)
    my_slot = lax.dynamic_index_in_dim(table_slot, my_index, 0, keepdims=False)
    my_target = my_owner * capacity + my_slot
    slot_ids = jnp.arange(capacity, dtype=jnp.int32)
    served = (table_owner == my_index)[:, :, None] & (
        table_slot[:, :, None] == slot_ids[None, None, :]
    )
    served_block = jnp.sum(jnp.where(served, table_offset[:, :, None], 0), axis=1).reshape(-1)
    served_used = jnp.any(served, axis=1).reshape(-1)
    outgoing = jnp.take(kv_blocks, served_block, axis=0)
    incoming = lax.all_to_all(outgoing, "ctx", split_axis=0, concat_axis=0, tiled=True)
    fetched = jnp.take(incoming, my_target, axis=0).reshape(blocks_here, NR, BS, 2 * head_cols)
    near_kv = jnp.concatenate([window, fetched], axis=1)
    near_groups = 3 + NR
    near_count = near_groups * BS
    query_heads = query_rows.reshape(blocks_here, BS, heads_here, DH)
    grad_heads = grad_rows.reshape(blocks_here, BS, heads_here, DH)
    near_keys = near_kv[..., :head_cols].reshape(blocks_here, near_groups, BS, heads_here, DH)
    near_values = near_kv[..., head_cols:].reshape(blocks_here, near_groups, BS, heads_here, DH)
    far_keys = global_kv[..., :head_cols].reshape(NG, BS, heads_here, DH)
    far_values = global_kv[..., head_cols:].reshape(NG, BS, heads_here, DH)
    scores = (
        jnp.concatenate(
            [
                jnp.einsum(
                    "bqhd,bgkhd->bhqgk", query_heads, near_keys, preferred_element_type=jnp.float32
                ).reshape(blocks_here, heads_here, BS, near_count),
                jnp.einsum(
                    "bqhd,gkhd->bhqgk", query_heads, far_keys, preferred_element_type=jnp.float32
                ).reshape(blocks_here, heads_here, BS, NG * BS),
            ],
            axis=3,
        )
        * inv_root
    )
    block_ids = my_index * blocks_here + jnp.arange(blocks_here, dtype=jnp.int32)
    usable = jnp.concatenate(
        [
            (block_ids > 0)[:, None],
            jnp.ones((blocks_here, 1), bool),
            (block_ids < total_blocks - 1)[:, None],
            jnp.ones((blocks_here, NR + NG), bool),
        ],
        axis=1,
    )
    column_ok = jnp.repeat(usable, BS, axis=1)[:, None, None, :]
    masked = jnp.where(column_ok, scores, -jnp.inf)
    row_max = jnp.max(masked, axis=3, keepdims=True)
    log_total = row_max + jnp.log(jnp.sum(jnp.exp(masked - row_max), axis=3, keepdims=True))
    probs_full = jnp.exp(masked - log_total)
    probs_half = probs_full.astype(jnp.bfloat16)
    near_probs = probs_half[..., :near_count].reshape(blocks_here, heads_here, BS, near_groups, BS)
    far_probs = probs_half[..., near_count:].reshape(blocks_here, heads_here, BS, NG, BS)
    outputs = jnp.einsum(
        "bhqgk,bgkhd->bqhd", near_probs, near_values, preferred_element_type=jnp.float32
    ) + jnp.einsum("bhqgk,gkhd->bqhd", far_probs, far_values, preferred_element_type=jnp.float32)
    row_dot = jnp.sum(grad_heads.astype(jnp.float32) * outputs, axis=3)
    dprobs = jnp.concatenate(
        [
            jnp.einsum(
                "bqhd,bgkhd->bhqgk", grad_heads, near_values, preferred_element_type=jnp.float32
            ).reshape(blocks_here, heads_here, BS, near_count),
            jnp.einsum(
                "bqhd,gkhd->bhqgk", grad_heads, far_values, preferred_element_type=jnp.float32
            ).reshape(blocks_here, heads_here, BS, NG * BS),
        ],
        axis=3,
    )
    dscores = probs_full * (dprobs - jnp.transpose(row_dot, (0, 2, 1))[..., None])
    ds_half = dscores.astype(jnp.bfloat16)
    near_ds = ds_half[..., :near_count].reshape(blocks_here, heads_here, BS, near_groups, BS)
    far_ds = ds_half[..., near_count:].reshape(blocks_here, heads_here, BS, NG, BS)
    query_grad = (
        (
            (
                jnp.einsum(
                    "bhqgk,bgkhd->bqhd", near_ds, near_keys, preferred_element_type=jnp.float32
                )
                + jnp.einsum(
                    "bhqgk,gkhd->bqhd", far_ds, far_keys, preferred_element_type=jnp.float32
                )
            )
            * inv_root
        )
        .astype(jnp.bfloat16)
        .reshape(tokens, head_cols)
    )

    def key_value_parts(ds_part, probs_part):
        key_part = (
            jnp.einsum(
                "bhqgk,bqhd->bgkhd", ds_part, query_heads, preferred_element_type=jnp.float32
            )
            * inv_root
        )
        value_part = jnp.einsum(
            "bhqgk,bqhd->bgkhd", probs_part, grad_heads, preferred_element_type=jnp.float32
        )
        out_shape = key_part.shape[:3] + (head_cols,)
        return jnp.concatenate([key_part.reshape(out_shape), value_part.reshape(out_shape)], axis=3)

    random_part = key_value_parts(near_ds[:, :, :, 3:], near_probs[:, :, :, 3:])
    random_part = random_part.astype(jnp.bfloat16).reshape(entries, BS, 2 * head_cols)
    back_rows = (
        jnp.zeros((devices * capacity, BS, 2 * head_cols), jnp.bfloat16)
        .at[my_target]
        .set(random_part)
    )
    arrived = lax.all_to_all(back_rows, "ctx", split_axis=0, concat_axis=0, tiled=True)
    window_part = key_value_parts(near_ds[:, :, :, :3], near_probs[:, :, :, :3])
    zero_block = jnp.zeros((1, BS, 2 * head_cols), jnp.float32)
    own_grad = (
        window_part[:, 1]
        + jnp.concatenate([window_part[1:, 0], zero_block], axis=0)
        + jnp.concatenate([zero_block, window_part[:-1, 2]], axis=0)
    )
    rims_out = jnp.concatenate([window_part[0, 0], window_part[blocks_here - 1, 2]], axis=0)
    rims_in = with_halo(rims_out.astype(jnp.bfloat16), (("ctx", 0),), BS).astype(rims_out.dtype)
    own_grad = own_grad.at[0].add(rims_in[:BS]).at[blocks_here - 1].add(rims_in[3 * BS :])
    far_key = (
        jnp.einsum("bhqgk,bqhd->gkhd", far_ds, query_heads, preferred_element_type=jnp.float32)
        * inv_root
    )
    far_value = jnp.einsum(
        "bhqgk,bqhd->gkhd", far_probs, grad_heads, preferred_element_type=jnp.float32
    )
    far_part = jnp.concatenate(
        [far_key.reshape(NG, BS, head_cols), far_value.reshape(NG, BS, head_cols)], axis=2
    )
    far_sum = lax.psum(far_part, "ctx")
    here_ids = jnp.arange(blocks_here, dtype=jnp.int32)
    own_global = (
        (global_owner == my_index)[None, :] & (global_offset[None, :] == here_ids[:, None])
    ).astype(jnp.float32)
    own_grad = own_grad + jnp.einsum(
        "jg,gkc->jkc", own_global, far_sum, precision=lax.Precision.HIGHEST
    )
    weights = (served_used[None, :] & (served_block[None, :] == here_ids[:, None])).astype(
        jnp.bfloat16
    )
    own_grad = own_grad + jnp.einsum(
        "jr,rkc->jkc", weights, arrived, preferred_element_type=jnp.float32
    )
    key_grad = own_grad[..., :head_cols].astype(jnp.bfloat16).reshape(tokens, head_cols)
    value_grad = own_grad[..., head_cols:].astype(jnp.bfloat16).reshape(tokens, head_cols)
    return (query_grad, key_grad, value_grad)


def solution(mesh):
    placed = (
        P(("ctx", "head"), None),
        P(("ctx", "head"), None),
        P(("ctx", "head"), None),
        P(("ctx", "head"), None),
        P(),
        P(),
    )
    return jax.shard_map(
        per_device,
        mesh=mesh,
        in_specs=placed,
        out_specs=(P("ctx", "head"), P("ctx", "head"), P("ctx", "head")),
        check_vma=False,
    )
```

profile of v0, /device:TPU:2, one launch (start us, length us, event | category | flops | bytes accessed | tf_op | source)
XLA Modules:
  0.0 762.3 jit_solution(3867168004326014338)
XLA Ops:
  7.2 1.6 copy.526
  8.8 9.2 %all-to-all-start = ((bf16[16,8,512]{2,0,1:T(8,128)(2,1)}), bf16[16,8,512]{2,0,1:T(8,128)(2,1)S(1)}, u32[]{:S(2)}, u32[]{:S(2)}) async-start(bf16[16,8,512]{2,0,1:T(8,128)(2,1)} %bitcast.216), calls=%async_computation | async-start | bytes 262144 | tf_op jit(solution)/shard_map/all_to_all | solution.py:34
  18.7 0.8 copy.297
  20.3 0.8 fusion.90
  22.7 4.7 all-to-all-start.1
  28.8 3.4 all-to-all-done.1
  32.1 4.7 all-to-all-start.3
  36.9 2.8 gather_fusion
  39.7 1.8 all-to-all-done.3
  41.6 4.7 all-to-all-start.4
  46.3 4.6 broadcast_select_fusion
  51.0 14.6 %all-to-all-start.2 = ((bf16[64,32,1024]{2,1,0:T(8,128)(2,1)}), bf16[64,32,1024]{2,1,0:T(8,128)(2,1)}, u32[]{:S(2)}, u32[]{:S(2)}) async-start(bf16[64,32,1024]{2,1,0:T(8,128)(2,1)} %broadcast_select_fusion), calls=%async_computation.2 | async-start | bytes 8388608 | tf_op jit(solution)/shard_map/all_to_all | solution.py:79
  79.1 0.7 fusion.72
  79.9 3.4 collective-permute-start
  83.3 1.5 collective-permute-start.1
  84.8 0.7 maximum_bitcast_fusion
  85.6 4.1 collective-permute-done.1
  89.7 0.8 pad_maximum_fusion.6
  90.5 298.1 %all-reduce.8.cloned.1.call-done = (bf16[1,32,1024]{2,1,0:T(8,128)(2,1)}, bf16[1,32,1024]{2,1,0:T(8,128)(2,1)}, bf16[1,32,1024]{2,1,0:T(8,128)(2,1)}, bf16[1,32,1024]{2,1,0:T(8,128)(2,1)}) async-done(((bf16[1,32,1024]{2,1,0:T(8,128)(2,1)}, bf16[1,32,1024]{2,1,0:T(8,128)(2,1)}, bf16[1,32,1024]{2,1,0:T(8,128)(2,1)}, bf16[1,32,1024]{2,1,0:T(8,128)(2,1)}), (bf16[1,32,1024]{2,1,0:T(8,128)(2,1)}, ...) | async-done | bytes 262160 | tf_op jit(solution)/shard_map/psum | solution.py:28
  388.5 0.8 constant_dynamic-update-slice_fusion.3
  389.4 0.8 constant_dynamic-update-slice_fusion.2
  390.2 0.8 constant_dynamic-update-slice_fusion.1
  391.1 0.8 constant_dynamic-update-slice_fusion
  391.9 0.8 slice_bitcast_fusion.8
  394.8 1.2 reshape.369
  396.0 2.8 gather_fusion.1
  399.2 1.3 slice_bitcast_fusion.1
  402.8 1.0 reshape.371
  404.3 1.2 fusion.92
  406.8 1.2 fusion.15
  408.6 0.9 concatenate.86
  410.0 1.5 fusion.24
  412.0 1.3 fusion.93
  414.5 2.5 broadcast_in_dim.69
  417.0 2.8 scatter_fusion
  419.9 9.1 %all-to-all-start.5 = ((bf16[64,32,1024]{2,1,0:T(8,128)(2,1)}), bf16[64,32,1024]{2,1,0:T(8,128)(2,1)}, u32[]{:S(2)}, u32[]{:S(2)}) async-start(bf16[64,32,1024]{2,1,0:T(8,128)(2,1)} %scatter_fusion), calls=%async_computation.5 | async-start | bytes 8388608 | tf_op jit(solution)/shard_map/all_to_all | solution.py:177
  429.5 1.7 slice.201
  431.7 0.8 reshape.436
  434.5 0.9 reshape.435
  435.3 1.9 pad_maximum_fusion.2
  438.7 3.5 collective-permute-start.2
  442.3 1.3 collective-permute-start.3
  445.3 3.3 collective-permute-done.3
  449.3 1.1 scatter-add.9
  450.3 164.0 %all-to-all-done.5 = bf16[64,32,1024]{2,1,0:T(8,128)(2,1)} async-done(((bf16[64,32,1024]{2,1,0:T(8,128)(2,1)}), bf16[64,32,1024]{2,1,0:T(8,128)(2,1)}, u32[]{:S(2)}, u32[]{:S(2)}) %all-to-all-start.5) | async-done | bytes 4194336 | tf_op jit(solution)/shard_map/all_to_all | solution.py:177
  614.3 6.7 fusion
  621.0 131.3 %all-reduce.6.cloned.1.call-done = f32[4,32,1024]{2,0,1:T(4,128)} async-done(((f32[4,32,1024]{2,0,1:T(4,128)}), f32[4,32,1024]{2,0,1:T(4,128)}) %all-reduce.6.cloned.1.call-update) | async-done | bytes 524304 | tf_op jit(solution)/shard_map/psum | solution.py:198
  752.3 1.7 fusion.5
  (170 shorter events, 24.7 us)
Async XLA Ops:
  7.2 14.2 %copy-start.19 = (bf16[16,4096]{1,0:T(8,128)(2,1)S(1)}, bf16[16,4096]{1,0:T(8,128)(2,1)}, u32[]{:S(2)}) copy-start(bf16[16,4096]{1,0:T(8,128)(2,1)} %param.12) | copy-start | bytes 393220
  7.2 20.3 %copy-start.20 = (bf16[16,4096]{1,0:T(8,128)(2,1)S(1)}, bf16[16,4096]{1,0:T(8,128)(2,1)}, u32[]{:S(2)}) copy-start(bf16[16,4096]{1,0:T(8,128)(2,1)} %param.10) | copy-start | bytes 393220
  7.2 20.9 %copy-start.21 = (bf16[16,4096]{1,0:T(8,128)(2,1)S(1)}, bf16[16,4096]{1,0:T(8,128)(2,1)}, u32[]{:S(2)}) copy-start(bf16[16,4096]{1,0:T(8,128)(2,1)} %param.13) | copy-start | bytes 393220
  8.8 13.9 %all-to-all-start = ((bf16[16,8,512]{2,0,1:T(8,128)(2,1)}), bf16[16,8,512]{2,0,1:T(8,128)(2,1)S(1)}, u32[]{:S(2)}, u32[]{:S(2)}) async-start(bf16[16,8,512]{2,0,1:T(8,128)(2,1)} %bitcast.216), calls=%async_computation | async-start | bytes 262144 | tf_op jit(solution)/shard_map/all_to_all | solution.py:34
  22.1 14.8 %copy-start.23 = (s32[64]{0:T(128)}, s32[64]{0:T(128)S(1)}, u32[]{:S(2)}) copy-start(s32[64]{0:T(128)S(1)} %reduce_sum.48) | copy-start | bytes 772
  22.7 9.4 %all-to-all-start.1 = ((bf16[16,8,512]{2,0,1:T(8,128)(2,1)}), bf16[16,8,512]{2,0,1:T(8,128)(2,1)S(1)}, u32[]{:S(2)}, u32[]{:S(2)}) async-start(bf16[16,8,512]{2,0,1:T(8,128)(2,1)} %bitcast.215), calls=%async_computation.1 | async-start | bytes 262144 | tf_op jit(solution)/shard_map/all_to_all | solution.py:35
  32.1 9.4 %all-to-all-start.3 = ((bf16[16,8,512]{2,0,1:T(8,128)(2,1)}), bf16[16,8,512]{2,0,1:T(8,128)(2,1)S(1)}, u32[]{:S(2)}, u32[]{:S(2)}) async-start(bf16[16,8,512]{2,0,1:T(8,128)(2,1)} %bitcast.214), calls=%async_computation.3 | async-start | bytes 262144 | tf_op jit(solution)/shard_map/all_to_all | solution.py:33
  41.6 9.4 %all-to-all-start.4 = ((bf16[16,8,512]{2,0,1:T(8,128)(2,1)}), bf16[16,8,512]{2,0,1:T(8,128)(2,1)S(1)}, u32[]{:S(2)}, u32[]{:S(2)}) async-start(bf16[16,8,512]{2,0,1:T(8,128)(2,1)} %bitcast.213), calls=%async_computation.4 | async-start | bytes 262144 | tf_op jit(solution)/shard_map/all_to_all | solution.py:36
  50.9 14.7 %copy-start.30 = (s32[4]{0:T(128)S(1)}, s32[4]{0:T(128)}, u32[]{:S(2)}) copy-start(s32[4]{0:T(128)} %param.15) | copy-start | bytes 52
  51.0 344.9 %all-to-all-start.2 = ((bf16[64,32,1024]{2,1,0:T(8,128)(2,1)}), bf16[64,32,1024]{2,1,0:T(8,128)(2,1)}, u32[]{:S(2)}, u32[]{:S(2)}) async-start(bf16[64,32,1024]{2,1,0:T(8,128)(2,1)} %broadcast_select_fusion), calls=%async_computation.2 | async-start | bytes 8388608 | tf_op jit(solution)/shard_map/all_to_all | solution.py:79
  65.6 322.9 %all-reduce.8.cloned.1.call-start = ((), (), s32[]{:S(2)}) async-start(), calls=%async_computation.7 | async-start | bytes 524288 | tf_op jit(solution)/shard_map/psum | solution.py:28
  78.5 12.0 %copy-start.26 = (s32[12]{0:T(128)}, s32[12]{0:T(128)S(1)}, u32[]{:S(2)}) copy-start(s32[12]{0:T(128)S(1)} %fusion.89) | copy-start | bytes 148
  79.9 320.6 %copy-start.3 = (bf16[4,32,4,128]{3,2,1,0:T(4,128)(2,1)}, bf16[4,32,4,128]{3,2,1,0:T(4,128)(2,1)S(1)}, u32[]{:S(2)}) copy-start(bf16[4,32,4,128]{3,2,1,0:T(4,128)(2,1)S(1)} %reshape.361) | copy-start | bytes 393220
  79.9 5.6 collective-permute-start
  83.3 6.4 collective-permute-start.1
  394.8 4.0 copy-start.28
  395.9 3.0 copy-start.13
  395.9 3.0 copy-start.14
  400.5 0.9 copy-start
  404.3 1.2 copy-start.2
  405.5 1.0 copy-start.5
  405.5 1.1 copy-start.18
  408.6 1.5 copy-start.22
  411.5 1.9 copy-start.12
  411.5 1.9 copy-start.4
  413.4 1.0 copy-start.11
  414.5 2.6 copy-start.27
  419.9 9.3 %copy-start.25 = (pred[256]{0:T(512)(128)(4,1)S(1)}, pred[256]{0:T(512)(128)(4,1)}, u32[]{:S(2)}) copy-start(pred[256]{0:T(512)(128)(4,1)} %get-tuple-element.33) | copy-start | bytes 772
  419.9 11.3 %copy-start.6 = (bf16[4,4,32,4,32]{4,3,2,1,0:T(4,128)(2,1)S(1)}, bf16[4,4,32,4,32]{4,3,2,1,0:T(4,128)(2,1)}, u32[]{:S(2)}) copy-start(bf16[4,4,32,4,32]{4,3,2,1,0:T(4,128)(2,1)} %reshape.371) | copy-start | bytes 393220
  419.9 194.4 %all-to-all-start.5 = ((bf16[64,32,1024]{2,1,0:T(8,128)(2,1)}), bf16[64,32,1024]{2,1,0:T(8,128)(2,1)}, u32[]{:S(2)}, u32[]{:S(2)}) async-start(bf16[64,32,1024]{2,1,0:T(8,128)(2,1)} %scatter_fusion), calls=%async_computation.5 | async-start | bytes 8388608 | tf_op jit(solution)/shard_map/all_to_all | solution.py:177
  428.9 3.6 copy-start.9
  428.9 323.4 %all-reduce.6.cloned.1.call-start = ((), (), s32[]{:S(2)}) async-start(), calls=%async_computation.6 | async-start | bytes 1048576 | tf_op jit(solution)/shard_map/psum | solution.py:198
  432.8 0.9 copy-start.16
  433.7 1.6 copy-start.15
  434.0 3.2 copy-start.7
  434.3 3.0 copy-start.10
  438.6 5.0 copy-start.8
  438.6 5.0 copy-start.17
  438.7 5.3 copy-start.1
  438.7 6.6 collective-permute-start.2
  442.3 6.4 collective-permute-start.3
  444.6 169.7 %copy-start.24 = (s32[64]{0:T(128)S(1)}, s32[64]{0:T(128)}, u32[]{:S(2)}) copy-start(s32[64]{0:T(128)} %copy-done.23) | copy-start | bytes 772
  450.3 302.0 %copy-start.29 = (pred[4]{0:T(512)(128)(4,1)S(1)}, pred[4]{0:T(512)(128)(4,1)}, u32[]{:S(2)}) copy-start(pred[4]{0:T(512)(128)(4,1)} %get-tuple-element.31) | copy-start | bytes 16
Sparse Core Ops, SparseCore 0:
  79.9 308.5 all-reduce.7
  437.4 314.8 all-reduce.5
where the time goes:
time: 764 us; the launch traced here: 762 us
  waiting for transfers between devices  607 us (79%)
  starting transfers between devices  57.1 us (7%)
  local copies, waits for them, and re-layouts  44 us (6%)
  between operations  25.1 us (3%)
  other arithmetic  15.6 us (2%)
  matrix products  13.9 us (2%)
    psum x1, waiting for transfers between devices, spread(): return lax.psum(jnp.where(mine, x, jnp.zeros_like(x)), axis)  298 us
    all_to_all x1, waiting for transfers between devices, per_device(): lax.all_to_all(back_rows, 'ctx', split_axis=0, concat_axis=0, tiled=True)  164 us
    psum x1, waiting for transfers between devices, per_device(): far_sum = lax.psum(far_part, 'ctx')  131 us
  transfers between devices with their start and end apart: 12, of which 9 were waited for; matrix products, arithmetic and copies ran while one was open for 6% of the time, Pallas kernels for 0%

commit v1 on v0

--- a/solution.py
+++ b/solution.py
@@ -195,7 +195,7 @@
     far_part = jnp.concatenate(
         [far_key.reshape(NG, BS, head_cols), far_value.reshape(NG, BS, head_cols)], axis=2
     )
-    far_sum = lax.psum(far_part, "ctx")
+    far_sum = jnp.sum(lax.all_gather(far_part, "ctx"), axis=0)
     here_ids = jnp.arange(blocks_here, dtype=jnp.int32)
     own_global = (
         (global_owner == my_index)[None, :] & (global_offset[None, :] == here_ids[:, None])

time: 764 us -> 888 us (1.16)
  the two profiles are of different devices: /device:TPU:2 before, /device:TPU:1 now
where the time goes in v1:
time: 888 us; the launch traced here: 886 us
  waiting for transfers between devices  716 us (81%)
  starting transfers between devices  56.8 us (6%)
  local copies, waits for them, and re-layouts  48.7 us (5%)
  between operations  24.7 us (3%)
  other arithmetic  24.6 us (3%)
  matrix products  15.2 us (2%)
    psum x1, waiting for transfers between devices, spread(): return lax.psum(jnp.where(mine, x, jnp.zeros_like(x)), axis)  290 us
    all_gather x1, waiting for transfers between devices, per_device(): far_sum = jnp.sum(lax.all_gather(far_part, 'ctx'), axis=0)  207 us
    all_to_all x1, waiting for transfers between devices, per_device(): lax.all_to_all(back_rows, 'ctx', split_axis=0, concat_axis=0, tiled=True)  206 us
  transfers between devices with their start and end apart: 12, of which 9 were waited for; matrix products, arithmetic and copies ran while one was open for 6% of the time, Pallas kernels for 0%

profile of v1, /device:TPU:1, one launch (start us, length us, event | category | flops | bytes accessed | tf_op | source)
XLA Modules:
  0.0 885.9 jit_solution(16244006457607217820)
XLA Ops:
  7.2 1.6 copy.523
  8.8 10.2 %all-to-all-start = ((bf16[16,8,512]{2,0,1:T(8,128)(2,1)}), bf16[16,8,512]{2,0,1:T(8,128)(2,1)S(1)}, u32[]{:S(2)}, u32[]{:S(2)}) async-start(bf16[16,8,512]{2,0,1:T(8,128)(2,1)} %bitcast.220), calls=%async_computation | async-start | bytes 262144 | tf_op jit(solution)/shard_map/all_to_all | solution.py:34
  20.5 1.6 copy.522
  24.2 4.5 all-to-all-start.1
  30.1 3.9 all-to-all-done.1
  34.0 4.1 all-to-all-start.4
  38.2 2.8 gather_fusion
  41.0 2.4 all-to-all-done.4
  43.5 4.1 all-to-all-start.3
  47.6 4.7 broadcast_select_fusion
  52.9 14.3 %all-to-all-start.2 = ((bf16[64,32,1024]{2,1,0:T(8,128)(2,1)}), bf16[64,32,1024]{2,1,0:T(8,128)(2,1)}, u32[]{:S(2)}, u32[]{:S(2)}) async-start(bf16[64,32,1024]{2,1,0:T(8,128)(2,1)} %broadcast_select_fusion), calls=%async_computation.2 | async-start | bytes 8388608 | tf_op jit(solution)/shard_map/all_to_all | solution.py:79
  80.7 2.8 collective-permute-start
  83.5 1.5 collective-permute-start.1
  85.1 4.0 collective-permute-done.1
  89.2 290.0 %all-reduce.5.cloned.1.call-done = (bf16[1,32,1024]{2,1,0:T(8,128)(2,1)}, bf16[1,32,1024]{2,1,0:T(8,128)(2,1)}, bf16[1,32,1024]{2,1,0:T(8,128)(2,1)}, bf16[1,32,1024]{2,1,0:T(8,128)(2,1)}) async-done(((bf16[1,32,1024]{2,1,0:T(8,128)(2,1)}, bf16[1,32,1024]{2,1,0:T(8,128)(2,1)}, bf16[1,32,1024]{2,1,0:T(8,128)(2,1)}, bf16[1,32,1024]{2,1,0:T(8,128)(2,1)}), (bf16[1,32,1024]{2,1,0:T(8,128)(2,1)}, ...) | async-done | bytes 262160 | tf_op jit(solution)/shard_map/psum | solution.py:28
  379.2 0.8 constant_dynamic-update-slice_fusion.3
  380.0 0.8 constant_dynamic-update-slice_fusion.2
  380.9 0.8 constant_dynamic-update-slice_fusion.1
  381.7 0.8 constant_dynamic-update-slice_fusion
  384.1 1.2 reshape.369
  386.6 2.8 gather_fusion.1
  389.8 1.4 slice_bitcast_fusion.1
  394.3 1.4 copy.320
  396.0 1.0 convolution_bitcast_fusion.3
  397.0 1.0 convolution_bitcast_fusion.6
  398.5 1.8 fusion.15
  401.9 1.2 copy.517
  404.8 1.2 fusion.93
  406.6 0.9 concatenate.86
  408.6 0.9 concatenate.85
  409.5 1.2 pad_maximum_fusion.1
  410.7 2.5 broadcast_in_dim.69
  413.3 2.8 scatter_fusion
  416.1 9.7 %all-to-all-start.5 = ((bf16[64,32,1024]{2,1,0:T(8,128)(2,1)}), bf16[64,32,1024]{2,1,0:T(8,128)(2,1)}, u32[]{:S(2)}, u32[]{:S(2)}) async-start(bf16[64,32,1024]{2,1,0:T(8,128)(2,1)} %scatter_fusion), calls=%async_computation.5 | async-start | bytes 8388608 | tf_op jit(solution)/shard_map/all_to_all | solution.py:177
  426.4 1.4 copy.390
  427.8 1.4 reshape.434
  429.6 1.4 copy.393
  431.0 2.4 reshape.435
  433.5 1.1 copy-done.1
  434.8 1.4 collective-permute-start.3
  436.2 4.0 collective-permute-start.2
  441.9 1.0 collective-permute-done.2
  443.5 1.1 scatter-add.9
  444.6 206.4 %all-to-all-done.5 = bf16[64,32,1024]{2,1,0:T(8,128)(2,1)} async-done(((bf16[64,32,1024]{2,1,0:T(8,128)(2,1)}), bf16[64,32,1024]{2,1,0:T(8,128)(2,1)}, u32[]{:S(2)}, u32[]{:S(2)}) %all-to-all-start.5) | async-done | bytes 4194336 | tf_op jit(solution)/shard_map/all_to_all | solution.py:177
  651.0 6.7 fusion
  657.7 207.2 %all-gather.3.cloned.1.call-done = f32[256,32,1024]{2,1,0:T(8,128)} async-done(((f32[4,32,1024]{2,1,0:T(8,128)}), f32[256,32,1024]{2,1,0:T(8,128)}) %all-gather.3.cloned.1.call-update) | async-done | bytes 33554448 | tf_op jit(solution)/shard_map/all_gather | solution.py:198
  864.9 11.8 %reduce_sum.61 = f32[4,32,1024]{2,1,0:T(8,128)S(1)} reduce(f32[64,4,32,1024]{3,2,1,0:T(8,128)} %bitcast.224, f32[]{:T(128)} %constant.169.clone.1), dimensions={0}, to_apply=%region_10.11 | reduce | flops 8257536 | bytes 34078724 | tf_op jit(solution)/shard_map/reduce_sum | solution.py:198
  876.7 1.0 fusion.5
  (149 shorter events, 26.0 us)
Async XLA Ops:
  7.2 21.6 %copy-start.11 = (bf16[16,4096]{1,0:T(8,128)(2,1)S(1)}, bf16[16,4096]{1,0:T(8,128)(2,1)}, u32[]{:S(2)}) copy-start(bf16[16,4096]{1,0:T(8,128)(2,1)} %param.13) | copy-start | bytes 393220
  7.2 22.3 %copy-start.12 = (bf16[16,4096]{1,0:T(8,128)(2,1)S(1)}, bf16[16,4096]{1,0:T(8,128)(2,1)}, u32[]{:S(2)}) copy-start(bf16[16,4096]{1,0:T(8,128)(2,1)} %param.10) | copy-start | bytes 393220
  8.8 15.4 %all-to-all-start = ((bf16[16,8,512]{2,0,1:T(8,128)(2,1)}), bf16[16,8,512]{2,0,1:T(8,128)(2,1)S(1)}, u32[]{:S(2)}, u32[]{:S(2)}) async-start(bf16[16,8,512]{2,0,1:T(8,128)(2,1)} %bitcast.220), calls=%async_computation | async-start | bytes 262144 | tf_op jit(solution)/shard_map/all_to_all | solution.py:34
  23.9 14.3 %copy-start.13 = (s32[64]{0:T(128)}, s32[64]{0:T(128)S(1)}, u32[]{:S(2)}) copy-start(s32[64]{0:T(128)S(1)} %reduce_sum.57) | copy-start | bytes 772
  24.2 9.8 %all-to-all-start.1 = ((bf16[16,8,512]{2,0,1:T(8,128)(2,1)}), bf16[16,8,512]{2,0,1:T(8,128)(2,1)S(1)}, u32[]{:S(2)}, u32[]{:S(2)}) async-start(bf16[16,8,512]{2,0,1:T(8,128)(2,1)} %bitcast.219), calls=%async_computation.1 | async-start | bytes 262144 | tf_op jit(solution)/shard_map/all_to_all | solution.py:35
  34.0 9.4 %all-to-all-start.4 = ((bf16[16,8,512]{2,0,1:T(8,128)(2,1)}), bf16[16,8,512]{2,0,1:T(8,128)(2,1)S(1)}, u32[]{:S(2)}, u32[]{:S(2)}) async-start(bf16[16,8,512]{2,0,1:T(8,128)(2,1)} %bitcast.217), calls=%async_computation.4 | async-start | bytes 262144 | tf_op jit(solution)/shard_map/all_to_all | solution.py:36
  43.5 9.4 %all-to-all-start.3 = ((bf16[16,8,512]{2,0,1:T(8,128)(2,1)}), bf16[16,8,512]{2,0,1:T(8,128)(2,1)S(1)}, u32[]{:S(2)}, u32[]{:S(2)}) async-start(bf16[16,8,512]{2,0,1:T(8,128)(2,1)} %bitcast.218), calls=%async_computation.3 | async-start | bytes 262144 | tf_op jit(solution)/shard_map/all_to_all | solution.py:33
  52.3 15.0 %copy-start.19 = (s32[4]{0:T(128)S(1)}, s32[4]{0:T(128)}, u32[]{:S(2)}) copy-start(s32[4]{0:T(128)} %param.15) | copy-start | bytes 52
  52.9 333.7 %all-to-all-start.2 = ((bf16[64,32,1024]{2,1,0:T(8,128)(2,1)}), bf16[64,32,1024]{2,1,0:T(8,128)(2,1)}, u32[]{:S(2)}, u32[]{:S(2)}) async-start(bf16[64,32,1024]{2,1,0:T(8,128)(2,1)} %broadcast_select_fusion), calls=%async_computation.2 | async-start | bytes 8388608 | tf_op jit(solution)/shard_map/all_to_all | solution.py:79
  67.2 312.0 %all-reduce.5.cloned.1.call-start = ((), (), s32[]{:S(2)}) async-start(), calls=%async_computation.7 | async-start | bytes 524288 | tf_op jit(solution)/shard_map/psum | solution.py:28
  79.8 0.9 copy-start.16
  80.6 784.3 %all-gather.3.cloned.1.call-start = ((), (), s32[]{:S(2)}) async-start(), calls=%async_computation.6 | async-start | bytes 34078720 | tf_op jit(solution)/shard_map/all_gather | solution.py:198
  80.7 4.4 collective-permute-start
  83.5 5.6 collective-permute-start.1
  392.4 1.6 copy-start
  393.2 0.7 copy-start.6
  395.7 1.3 copy-start.10
  395.7 2.2 slice-start
  398.5 1.8 copy-start.4
  398.5 1.8 copy-start.8
  400.8 0.7 copy-start.7
  401.9 2.3 copy-start.2
  403.4 1.0 slice-start.1
  410.7 2.6 copy-start.17
  416.1 9.7 %copy-start.15 = (pred[256]{0:T(512)(128)(4,1)S(1)}, pred[256]{0:T(512)(128)(4,1)}, u32[]{:S(2)}) copy-start(pred[256]{0:T(512)(128)(4,1)} %get-tuple-element.33) | copy-start | bytes 772
  416.1 234.9 %all-to-all-start.5 = ((bf16[64,32,1024]{2,1,0:T(8,128)(2,1)}), bf16[64,32,1024]{2,1,0:T(8,128)(2,1)}, u32[]{:S(2)}, u32[]{:S(2)}) async-start(bf16[64,32,1024]{2,1,0:T(8,128)(2,1)} %scatter_fusion), calls=%async_computation.5 | async-start | bytes 8388608 | tf_op jit(solution)/shard_map/all_to_all | solution.py:177
  426.4 2.9 copy-start.5
  433.4 1.1 copy-start.1
  434.6 5.6 copy-start.3
  434.6 5.6 copy-start.9
  434.8 7.1 collective-permute-start.3
  436.2 6.7 collective-permute-start.2
  441.2 209.7 %copy-start.14 = (s32[64]{0:T(128)S(1)}, s32[64]{0:T(128)}, u32[]{:S(2)}) copy-start(s32[64]{0:T(128)} %copy-done.13) | copy-start | bytes 772
  864.9 11.8 %copy-start.18 = (pred[4]{0:T(512)(128)(4,1)S(1)}, pred[4]{0:T(512)(128)(4,1)}, u32[]{:S(2)}) copy-start(pred[4]{0:T(512)(128)(4,1)} %get-tuple-element.31) | copy-start | bytes 16
Sparse Core Ops, SparseCore 0:
  80.7 298.4 all-reduce.4
  404.4 460.4 all-gather.2
